TPU v7x, 32 devices: a whole 2x2x4 slice. The times are simulated.
32 devices in a mesh: groups: 2 (over x), ctx: 16 (over z, y, core).
Axes of the slice: x: 2, y: 2, z: 4, core: 2. Of those that a mesh axis runs over, the one named last changes fastest.
Arguments:
- tokens: bfloat16 [8192, 2048], P(('groups', 'ctx')), parts along dimension 0, may hold values from -6 to 6
- kernel: float32 [3, 2048], replicated, may hold values from -3 to 3
- w_query: bfloat16 [2048, 256], P('ctx'), may hold values from -0.125 to 0.125
- w_key: bfloat16 [2048, 256], P('ctx'), may hold values from -0.125 to 0.125
- w_value: bfloat16 [2048, 1024], P('ctx'), may hold values from -0.125 to 0.125
- cotangent: bfloat16 [8192, 1024], P(('groups', 'ctx')), parts along dimension 0, may hold values from -6 to 6
Outputs:
- mixed: bfloat16 [8192, 1024], P(('groups', 'ctx')), parts along dimension 0
- grad_tokens: bfloat16 [8192, 2048], P(('groups', 'ctx')), parts along dimension 0
- grad_query: float32 [4096, 256], P(('groups', 'ctx')), parts along dimension 0
- grad_key: float32 [4096, 256], P(('groups', 'ctx')), parts along dimension 0
- grad_value: float32 [4096, 1024], P(('groups', 'ctx')), parts along dimension 0
- grad_kernel: float32 [6, 2048], P('groups', 'ctx'), parts along dimension 0
There are 2 independent parts, one for each index of `groups`. A program takes and returns all parts, laid end to end along the dimension named above; an argument that names none is the same for every part. Nothing has to cross between parts.
All inputs are finite; a program needn't handle non-finite values.
Results may differ from a plain program's by a relative error of at most 0.009.
Values may be sent and summed in bfloat16 or wider, within the bound.
No kernel may reach another device: no remote copies, remote signals or barrier semaphores. Data moves between devices by JAX's collectives and lax.ppermute only.
A program may use at most 128 MiB of HBM per device.

v0:
```python
import jax
import jax.numpy as jnp
import numpy as np
from jax import lax
from jax.sharding import PartitionSpec as P

HEADS = 16
FEAT = 16
HEAD_DIM = 64


def from_behind(value, axis, steps):
    count = lax.axis_size(axis)
    first, last = (max(0, -steps), min(count, count - steps))
    return lax.ppermute(value, axis, [(source, source + steps) for source in range(first, last)])


def pair_tables(feat):
    rows, cols = np.triu_indices(feat)
    coef = np.where(rows == cols, 1.0 / np.sqrt(2.0 * feat), 1.0 / np.sqrt(1.0 * feat))
    return (rows, cols, coef)


def features(block):
    feat = block.shape[-1]
    rows, cols, coef = pair_tables(feat)
    scale = jnp.asarray(coef, jnp.float32)
    eye = np.eye(feat, dtype=np.float32)
    high = lax.Precision.HIGHEST
    pick_rows = jnp.einsum("...f,fp->...p", block, jnp.asarray(eye[:, rows]), precision=high)
    pick_cols = jnp.einsum("...f,fp->...p", block, jnp.asarray(eye[:, cols]), precision=high)
    quad = pick_rows * pick_cols * scale
    ones = jnp.ones(block.shape[:-1] + (1,), jnp.float32)
    return jnp.concatenate((ones, block * feat ** (-0.25), quad), axis=-1)


def block_attend(query, key, value, state, norm):
    length, heads, feat = query.shape
    hdim = value.shape[2]
    width = state.shape[0]
    high = lax.Precision.HIGHEST
    sigma = jnp.einsum("thf,shf->hts", query, key, precision=high) / np.sqrt(1.0 * feat)
    weight = 1.0 + sigma + 0.5 * sigma * sigma
    causal = lax.broadcasted_iota(jnp.int32, (length, length), 0) >= lax.broadcasted_iota(
        jnp.int32, (length, length), 1
    )
    weight = jnp.where(causal[None], weight, jnp.float32(0.0))
    numer = jnp.einsum("hts,she->the", weight, value, precision=high)
    denom = jnp.sum(weight, axis=2).T
    phi_query = features(query)
    numer = numer + jnp.einsum(
        "thn,nhe->the", phi_query, state.reshape(width, heads, hdim), precision=high
    )
    denom = denom + jnp.einsum("thn,nh->th", phi_query, norm, precision=high)
    attended = numer / denom[:, :, None]
    scaled = attended * lax.rsqrt(jnp.mean(attended * attended, axis=2, keepdims=True) + 1e-06)
    return scaled.reshape(length, heads * hdim)


def block_state(key, value):
    length, heads, hdim = value.shape
    phi_key = features(key)
    state = jnp.einsum("shn,she->nhe", phi_key, value, precision=lax.Precision.HIGHEST)
    return (state.reshape(phi_key.shape[2], heads * hdim), jnp.sum(phi_key, axis=0).T)


def pack_parts(state, norm, devices):
    flat = jnp.concatenate((state.reshape(-1), norm.reshape(-1)), axis=0)
    total = flat.shape[0]
    piece = -(-total // (devices * 128)) * 128
    flat = jnp.concatenate((flat, jnp.zeros((devices * piece - total,), jnp.float32)), axis=0)
    return flat.reshape(devices, piece)


def unpack_parts(parts, state, norm):
    flat = parts.reshape(-1)
    count = state.size
    new_state = flat[:count].reshape(state.shape)
    new_norm = flat[count : count + norm.size].reshape(norm.shape)
    return (new_state, new_norm)


def before_sum(block):
    zero_row = jnp.zeros((1, block.shape[1]), jnp.float32)
    return jnp.concatenate((zero_row, jnp.cumsum(block, axis=0)[:-1]), axis=0)


def after_sum(block):
    zero_row = jnp.zeros((1, block.shape[1]), jnp.float32)
    return jnp.concatenate((lax.cumsum(block[1:], axis=0, reverse=True), zero_row), axis=0)


def exclusive_scan(parts, axis, direction):
    count = lax.axis_size(axis)
    total = parts
    step = 1
    while step < count:
        if direction > 0:
            pairs = [(source, source + step) for source in range(count - step)]
        else:
            pairs = [(source + step, source) for source in range(count - step)]
        moved = lax.ppermute(total, axis, pairs)
        total = jax.tree.map(jnp.add, total, moved)
        step *= 2
    return jax.tree.map(jnp.subtract, total, parts)


def local_gate(tokens_f, rim_f, kernel):
    padded = jnp.concatenate((rim_f, tokens_f), axis=0)
    conv = kernel[0] * padded[2:] + kernel[1] * padded[1:-1] + kernel[2] * padded[:-2]
    return tokens_f + jax.nn.sigmoid(tokens_f) * conv


def body(tokens, kernel, w_query, w_key, w_value, cotangent):
    length = tokens.shape[0]
    qk_cols = w_query.shape[1]
    devices = lax.axis_size("ctx")
    rim = from_behind(tokens[length - 2 :], "ctx", 1)
    tokens_f = tokens.astype(jnp.float32)
    rim_f = rim.astype(jnp.float32)
    gated = local_gate(tokens_f, rim_f, kernel).astype(jnp.bfloat16)
    stacked = lax.all_gather(
        jnp.concatenate((w_query, w_key, w_value), axis=1), "ctx", axis=0, tiled=True
    )
    full_qk = stacked[:, : 2 * qk_cols]
    full_v = stacked[:, 2 * qk_cols :]
    proj_qk = jnp.dot(gated, full_qk, preferred_element_type=jnp.float32).astype(jnp.bfloat16)
    proj_v = jnp.dot(gated, full_v, preferred_element_type=jnp.float32).astype(jnp.bfloat16)
    query_f = proj_qk[:, :qk_cols].astype(jnp.float32).reshape(length, HEADS, FEAT)
    key_f = proj_qk[:, qk_cols:].astype(jnp.float32).reshape(length, HEADS, FEAT)
    value_f = proj_v.astype(jnp.float32).reshape(length, HEADS, HEAD_DIM)
    own_state, own_norm = block_state(key_f, value_f)
    prev_state, prev_norm = exclusive_scan((own_state, own_norm), "ctx", 1)
    out_f, back = jax.vjp(block_attend, query_f, key_f, value_f, prev_state, prev_norm)
    mixed = out_f.astype(jnp.bfloat16)
    d_query, d_key, d_value, d_state, d_norm = back(cotangent.astype(jnp.float32))
    d_query = d_query.reshape(length, qk_cols).astype(jnp.bfloat16)
    query_part = lax.dot_general(
        gated, d_query, (((0,), (0,)), ((), ())), preferred_element_type=jnp.float32
    )
    query_part, d_state, d_norm = lax.optimization_barrier((query_part, d_state, d_norm))
    grad_query = lax.psum_scatter(query_part, "ctx", scatter_dimension=0, tiled=True)
    later_state, later_norm = exclusive_scan((d_state, d_norm), "ctx", -1)
    later_state, later_norm, grad_query = lax.optimization_barrier((later_state, later_norm, grad_query))
    _, back_state = jax.vjp(block_state, key_f, value_f)
    extra_key, extra_value = back_state((later_state, later_norm))
    d_key = (d_key + extra_key).reshape(length, qk_cols).astype(jnp.bfloat16)
    d_value = (d_value + extra_value).reshape(length, HEADS * HEAD_DIM).astype(jnp.bfloat16)
    d_kv = jnp.concatenate((d_key, d_value), axis=1)
    grads = lax.psum_scatter(
        lax.dot_general(gated, d_kv, (((0,), (0,)), ((), ())), preferred_element_type=jnp.float32),
        "ctx",
        scatter_dimension=0,
        tiled=True,
    )
    contract = (((1,), (1,)), ((), ()))
    d_gated = lax.dot_general(
        jnp.concatenate((d_query, d_key), axis=1), full_qk, contract, preferred_element_type=jnp.float32
    )
    d_gated = d_gated + lax.dot_general(d_value, full_v, contract, preferred_element_type=jnp.float32)
    _, back_conv = jax.vjp(local_gate, tokens_f, rim_f, kernel)
    d_tokens, d_rim, d_kernel = back_conv(d_gated)
    carried = from_behind(d_rim, "ctx", -1)
    d_tokens = jnp.concatenate((d_tokens[: length - 2], d_tokens[length - 2 :] + carried), axis=0)
    taps, width = d_kernel.shape
    d_kernel = d_kernel.reshape(taps, devices, width // devices).transpose(1, 0, 2)
    kernel_share = lax.psum_scatter(
        d_kernel.reshape(devices * taps, width // devices), "ctx", scatter_dimension=0, tiled=True
    )
    return (
        mixed,
        d_tokens.astype(jnp.bfloat16),
        grad_query,
        grads[:, :qk_cols],
        grads[:, qk_cols:],
        kernel_share,
    )


def solution(mesh):
    in_specs = (
        P(("groups", "ctx"), None),
        P(),
        P("ctx", None),
        P("ctx", None),
        P("ctx", None),
        P(("groups", "ctx"), None),
    )
    out_specs = (
        P(("groups", "ctx"), None),
        P(("groups", "ctx"), None),
        P(("groups", "ctx"), None),
        P(("groups", "ctx"), None),
        P(("groups", "ctx"), None),
        P("groups", "ctx"),
    )
    return jax.shard_map(body, mesh=mesh, in_specs=in_specs, out_specs=out_specs, check_vma=False)
```

profile of v0, /device:TPU:0, one launch (start us, length us, event | category | flops | bytes accessed | tf_op | source)
XLA Modules:
  0.0 478.5 jit_solution(3057746682918400952)
XLA Ops:
  17.2 58.3 %all-gather.2.cloned.1.call-done = bf16[2048,1536]{1,0:T(8,128)(2,1)} async-done(((bf16[128,1536]{1,0:T(8,128)(2,1)}), bf16[2048,1536]{1,0:T(8,128)(2,1)}) %all-gather.2.cloned.1.call-update) | async-done | bytes 6291472 | tf_op jit(solution)/shard_map/all_gather | solution.py:122
  86.3 3.4 fusion.29
  90.8 6.8 %multiply_multiply_fusion = (f32[256,16,136]{0,2,1:T(8,128)}, f32[256,16,136]{0,2,1:T(8,128)S(1)}, f32[256,16,136]{0,2,1:T(8,128)}) fusion(f32[256,16,136]{0,2,1:T(8,128)} %fusion.105, f32[136]{0:T(256)} %constant.31.clone, f32[256,16,136]{0,2,1:T(8,128)} %fusion.103, f32[256,16,136]{0,2,1:T(8,128)} %fusion.104, bf16[256,16,16]{0,2,1:T(8,128)(2,1)} %bitcast.137, ...), kind=kOutput, calls=%fused_computation.24 | convolution fusion | flops 109182976 | bytes 13509664 | tf_op jit(solution)/shard_map/jvp(...f,fp->...p)/dot_general | solution.py:30
  108.9 11.3 %collective-permute-start.2 = (f32[153,1024]{1,0:T(8,128)}, f32[153,1024]{1,0:T(8,128)}, u32[]{:S(2)}, u32[]{:S(2)}) collective-permute-start(f32[153,1024]{1,0:T(8,128)} %add.135), channel_id=1, source_target_pairs={{0,2},{1,3},{2,4},{3,5},{4,6},{5,7},{6,8},{7,9},{8,10},{9,11},{10,... | collective-permute-start | bytes 1880072 | tf_op jit(solution)/shard_map/ppermute | solution.py:102
  124.8 14.2 %collective-permute-start.6 = (f32[153,16]{0,1:T(8,128)}, f32[153,16]{0,1:T(8,128)}, u32[]{:S(2)}, u32[]{:S(2)}) collective-permute-start(f32[153,16]{0,1:T(8,128)} %bitcast_add_fusion.1), channel_id=1, source_target_pairs={{0,2},{1,3},{2,4},{3,5},{4,6},{5,7},{6,8},{7,9},{8,10},{9,11},{10,... | collective-permute-start | bytes 29384 | tf_op jit(solution)/shard_map/ppermute | solution.py:102
  146.8 3.3 collective-permute-start.3
  155.5 3.6 fusion.57
  162.8 4.3 collective-permute-start.4
  168.5 3.3 fusion.82
  172.5 5.6 %collective-permute-done.4 = f32[153,1024]{1,0:T(8,128)S(1)} collective-permute-done((f32[153,1024]{1,0:T(8,128)S(1)}, f32[153,1024]{1,0:T(8,128)S(1)}, u32[]{:S(2)}, u32[]{:S(2)}) %collective-permute-start.4) | collective-permute-done | bytes 626720 | tf_op jit(solution)/shard_map/ppermute | solution.py:102
  181.5 4.9 %multiply_reduce_fusion.4 = (f32[256,16]{0,1:T(8,128)S(1)}, f32[256,16]{0,1:T(8,128)S(1)}, f32[256,16,64]{0,2,1:T(8,128)S(1)}) fusion(f32[256,1024]{0,1:T(8,128)} %copy.85, f32[256,16]{0,1:T(8,128)} %get-tuple-element.49, f32[16,64,256]{2,1,0:T(8,128)} %fusion.57, f32[153,16,64]{0,2,1:T(8,128)} %bitcast.134, f32[256,16,136]{0,2,1:T(8,128)} %get-tuple-element.69, ...), kind=kOutput, calls=%fused_computation.81 | convolution fusion | flops 484114432 | bytes 6312548 | tf_op jit(solution)/shard_map/jvp(thn,nhe->the)/dot_general | solution.py:51
  191.2 4.0 fusion.63
  195.3 3.4 fusion.1
  218.8 15.5 %collective-permute-done.10 = f32[153,1024]{1,0:T(8,128)S(1)} collective-permute-done((f32[153,1024]{1,0:T(8,128)S(1)}, f32[153,1024]{1,0:T(8,128)S(1)}, u32[]{:S(2)}, u32[]{:S(2)}) %collective-permute-start.10) | collective-permute-done | bytes 626720 | tf_op jit(solution)/shard_map/ppermute | solution.py:102
  237.0 15.9 %collective-permute-done.13 = f32[153,16]{0,1:T(8,128)S(1)} collective-permute-done((f32[153,16]{0,1:T(8,128)S(1)}, f32[153,16]{0,1:T(8,128)S(1)}, u32[]{:S(2)}, u32[]{:S(2)}) %collective-permute-start.13) | collective-permute-done | bytes 9824 | tf_op jit(solution)/shard_map/ppermute | solution.py:102
  254.2 12.7 %collective-permute-done.14 = f32[153,16]{0,1:T(8,128)S(1)} collective-permute-done((f32[153,16]{0,1:T(8,128)S(1)}, f32[153,16]{0,1:T(8,128)S(1)}, u32[]{:S(2)}, u32[]{:S(2)}) %collective-permute-start.14) | collective-permute-done | bytes 9824 | tf_op jit(solution)/shard_map/ppermute | solution.py:102
  268.3 20.2 %collective-permute-done.15 = f32[153,16]{0,1:T(8,128)S(1)} collective-permute-done((f32[153,16]{0,1:T(8,128)S(1)}, f32[153,16]{0,1:T(8,128)S(1)}, u32[]{:S(2)}, u32[]{:S(2)}) %collective-permute-start.15) | collective-permute-done | bytes 9824 | tf_op jit(solution)/shard_map/ppermute | solution.py:102
  291.6 5.7 %fusion.55 = f32[16,64,256]{2,1,0:T(8,128)} fusion(f32[16,256,256]{1,2,0:T(8,128)S(1)} %copy-done.67, pred[256,256]{0,1:T(8,128)(4,1)S(1)} %copy-done.57, f32[256,16,64]{0,2,1:T(8,128)S(1)} %copy-done.13), kind=kOutput, calls=%fused_computation.66 | convolution fusion | flops 811597824 | bytes 6356992 | tf_op jit(solution)/shard_map/transpose(jvp(hts,she->the))/dot_general | solution.py:48
  297.8 27.1 %collective-permute-done.12 = f32[153,1024]{1,0:T(8,128)S(1)} collective-permute-done((f32[153,1024]{1,0:T(8,128)S(1)}, f32[153,1024]{1,0:T(8,128)S(1)}, u32[]{:S(2)}, u32[]{:S(2)}) %collective-permute-start.12) | collective-permute-done | bytes 626720 | tf_op jit(solution)/shard_map/ppermute | solution.py:102
  343.5 5.6 %fusion.70 = f32[2048,1280]{1,0:T(8,128)} fusion(bf16[256,2048]{1,0:T(8,128)(2,1)S(1)} %add_convert_fusion, bf16[256,1024]{0,1:T(8,128)(2,1)S(1)} %bitcast.145, bf16[256,256]{0,1:T(8,128)(2,1)S(1)} %bitcast.153), kind=kOutput, calls=%fused_computation.87 | convolution fusion | flops 1343488000 | bytes 12189696 | tf_op jit(solution)/shard_map/dot_general | solution.py:151
  352.1 4.0 fusion.2
  356.2 5.3 %multiply_reduce_fusion.2 = (f32[2048]{0:T(1024)S(1)}, f32[2048]{0:T(1024)S(1)}, f32[2048]{0:T(1024)S(1)}, f32[256,2048]{1,0:T(8,128)}, f32[256,2048]{1,0:T(8,128)}) fusion(f32[256,2048]{1,0:T(8,128)S(1)} %copy-done.6, f32[2,2048]{1,0:T(2,128)S(1)} %copy-done.43, bf16[256,2048]{1,0:T(8,128)(2,1)S(1)} %copy-done.11, f32[256,2048]{1,0:T(8,128)S(1)} %fusion.2, ...), kind=kOutput, calls=%fused_computation.37 | convolution fusion | flops 544729088 | bytes 11837440 | tf_op jit(solution)/shard_map/dot_general | solution.py:157
  367.6 62.0 %all-reduce.6 = f32[48,128]{1,0:T(8,128)S(1)} all-reduce(f32[48,128]{1,0:T(8,128)S(1)} %reshape.119), channel_id=4, replica_groups=mesh['groups'=2,'ctx'=16] {'ctx'}, use_global_device_ids=true, to_apply=%region_10.11.clone | all-reduce | flops 6144 | bytes 49152
  436.4 31.7 %reduce-scatter.5.cloned.1.call-done = f32[128,1280]{1,0:T(8,128)} async-done(((f32[2048,1280]{1,0:T(8,128)}), f32[128,1280]{1,0:T(8,128)}) %reduce-scatter.5.cloned.1.call-update) | async-done | bytes 655376 | tf_op jit(solution)/shard_map/reduce_scatter | solution.py:150
  (243 shorter events, 130.3 us)
Async XLA Ops:
  7.2 68.3 %all-gather.2.cloned.1.call-start = ((), (), s32[]{:S(2)}) async-start(), calls=%async_computation.2 | async-start | bytes 6684672 | tf_op jit(solution)/shard_map/all_gather | solution.py:122
  9.1 316.9 %reduce-scatter.3.cloned.1.call-start = ((), (), s32[]{:S(2)}) async-start(), calls=%async_computation.3 | async-start | bytes 2228224 | tf_op jit(solution)/shard_map/reduce_scatter | solution.py:142
  9.9 5.4 %collective-permute-start = (bf16[2,2048]{1,0:T(2,128)(2,1)S(1)}, bf16[2,2048]{1,0:T(2,128)(2,1)S(1)}, u32[]{:S(2)}, u32[]{:S(2)}) collective-permute-start(bf16[2,2048]{1,0:T(2,128)(2,1)S(1)} %slice.50), channel_id=1, source_target_pairs={{0,1},{1,2},{2,3},{3,4},{4,5},{5,6},{6,7},{7,8},{8,9},{9,10},{10,1... | collective-permute-start | bytes 24584 | tf_op jit(solution)/shard_map/ppermute | solution.py:15
  102.9 4.1 collective-permute-start.1
  108.9 35.6 %collective-permute-start.2 = (f32[153,1024]{1,0:T(8,128)}, f32[153,1024]{1,0:T(8,128)}, u32[]{:S(2)}, u32[]{:S(2)}) collective-permute-start(f32[153,1024]{1,0:T(8,128)} %add.135), channel_id=1, source_target_pairs={{0,2},{1,3},{2,4},{3,5},{4,6},{5,7},{6,8},{7,9},{8,10},{9,11},{10,... | collective-permute-start | bytes 1880072 | tf_op jit(solution)/shard_map/ppermute | solution.py:102
  121.6 2.6 collective-permute-start.5
  124.8 17.0 %collective-permute-start.6 = (f32[153,16]{0,1:T(8,128)}, f32[153,16]{0,1:T(8,128)}, u32[]{:S(2)}, u32[]{:S(2)}) collective-permute-start(f32[153,16]{0,1:T(8,128)} %bitcast_add_fusion.1), channel_id=1, source_target_pairs={{0,2},{1,3},{2,4},{3,5},{4,6},{5,7},{6,8},{7,9},{8,10},{9,11},{10,... | collective-permute-start | bytes 29384 | tf_op jit(solution)/shard_map/ppermute | solution.py:102
  142.6 10.4 %collective-permute-start.7 = (f32[153,16]{0,1:T(8,128)S(1)}, f32[153,16]{0,1:T(8,128)S(1)}, u32[]{:S(2)}, u32[]{:S(2)}) collective-permute-start(f32[153,16]{0,1:T(8,128)S(1)} %add.142), channel_id=1, source_target_pairs={{0,4},{1,5},{2,6},{3,7},{4,8},{5,9},{6,10},{7,11},{8,12},{9,13},{1... | collective-permute-start | bytes 29384 | tf_op jit(solution)/shard_map/ppermute | solution.py:102
  146.8 14.7 %collective-permute-start.3 = (f32[153,1024]{1,0:T(8,128)}, f32[153,1024]{1,0:T(8,128)}, u32[]{:S(2)}, u32[]{:S(2)}) collective-permute-start(f32[153,1024]{1,0:T(8,128)} %add.136), channel_id=1, source_target_pairs={{0,4},{1,5},{2,6},{3,7},{4,8},{5,9},{6,10},{7,11},{8,12},{9,13},{1... | collective-permute-start | bytes 1880072 | tf_op jit(solution)/shard_map/ppermute | solution.py:102
  153.6 13.6 %collective-permute-start.8 = (f32[153,16]{0,1:T(8,128)}, f32[153,16]{0,1:T(8,128)}, u32[]{:S(2)}, u32[]{:S(2)}) collective-permute-start(f32[153,16]{0,1:T(8,128)} %add.143), channel_id=1, source_target_pairs={{0,8},{1,9},{2,10},{3,11},{4,12},{5,13},{6,14},{7,15},{16,24},{17,... | collective-permute-start | bytes 29384 | tf_op jit(solution)/shard_map/ppermute | solution.py:102
  162.8 15.2 %collective-permute-start.4 = (f32[153,1024]{1,0:T(8,128)S(1)}, f32[153,1024]{1,0:T(8,128)S(1)}, u32[]{:S(2)}, u32[]{:S(2)}) collective-permute-start(f32[153,1024]{1,0:T(8,128)S(1)} %add.137), channel_id=1, source_target_pairs={{0,8},{1,9},{2,10},{3,11},{4,12},{5,13},{6,14},{7,15},{16,24},{17,... | collective-permute-start | bytes 1880072 | tf_op jit(solution)/shard_map/ppermute | solution.py:102
  209.3 258.9 %reduce-scatter.5.cloned.1.call-start = ((), (), s32[]{:S(2)}) async-start(), calls=%async_computation.4 | async-start | bytes 11141120 | tf_op jit(solution)/shard_map/reduce_scatter | solution.py:150
  211.7 4.3 collective-permute-start.9
  216.0 75.5 %copy-start.67 = (f32[16,256,256]{1,2,0:T(8,128)S(1)}, f32[16,256,256]{1,2,0:T(8,128)}, u32[]{:S(2)}) copy-start(f32[16,256,256]{1,2,0:T(8,128)} %copy-done.65) | copy-start | bytes 12582916
  217.3 74.2 %copy-start.13 = (f32[256,16,64]{0,2,1:T(8,128)S(1)}, f32[256,16,64]{0,2,1:T(8,128)}, u32[]{:S(2)}) copy-start(f32[256,16,64]{0,2,1:T(8,128)} %copy-done.12) | copy-start | bytes 3145732
  217.3 74.2 %copy-start.57 = (pred[256,256]{0,1:T(8,128)(4,1)S(1)}, pred[256,256]{0,1:T(8,128)(4,1)}, u32[]{:S(2)}) copy-start(pred[256,256]{0,1:T(8,128)(4,1)} %iota_compare_fusion) | copy-start | bytes 196612
  217.4 17.0 %collective-permute-start.10 = (f32[153,1024]{1,0:T(8,128)S(1)}, f32[153,1024]{1,0:T(8,128)S(1)}, u32[]{:S(2)}, u32[]{:S(2)}) collective-permute-start(f32[153,1024]{1,0:T(8,128)S(1)} %add.149), channel_id=1, source_target_pairs={{2,0},{3,1},{4,2},{5,3},{6,4},{7,5},{8,6},{9,7},{10,8},{11,9},{12,... | collective-permute-start | bytes 1880072 | tf_op jit(solution)/shard_map/ppermute | solution.py:102
  234.4 55.4 %collective-permute-start.11 = (f32[153,1024]{1,0:T(8,128)S(1)}, f32[153,1024]{1,0:T(8,128)S(1)}, u32[]{:S(2)}, u32[]{:S(2)}) collective-permute-start(f32[153,1024]{1,0:T(8,128)S(1)} %add.150), channel_id=1, source_target_pairs={{4,0},{5,1},{6,2},{7,3},{8,4},{9,5},{10,6},{11,7},{12,8},{13,9},{1... | collective-permute-start | bytes 1880072 | tf_op jit(solution)/shard_map/ppermute | solution.py:102
  235.7 17.2 %collective-permute-start.13 = (f32[153,16]{0,1:T(8,128)S(1)}, f32[153,16]{0,1:T(8,128)S(1)}, u32[]{:S(2)}, u32[]{:S(2)}) collective-permute-start(f32[153,16]{0,1:T(8,128)S(1)} %bitcast.156), channel_id=1, source_target_pairs={{1,0},{2,1},{3,2},{4,3},{5,4},{6,5},{7,6},{8,7},{9,8},{10,9},{11,1... | collective-permute-start | bytes 29384 | tf_op jit(solution)/shard_map/ppermute | solution.py:102
  253.0 14.0 %collective-permute-start.14 = (f32[153,16]{0,1:T(8,128)S(1)}, f32[153,16]{0,1:T(8,128)S(1)}, u32[]{:S(2)}, u32[]{:S(2)}) collective-permute-start(f32[153,16]{0,1:T(8,128)S(1)} %add.153), channel_id=1, source_target_pairs={{2,0},{3,1},{4,2},{5,3},{6,4},{7,5},{8,6},{9,7},{10,8},{11,9},{12,... | collective-permute-start | bytes 29384 | tf_op jit(solution)/shard_map/ppermute | solution.py:102
  267.0 21.5 %collective-permute-start.15 = (f32[153,16]{0,1:T(8,128)S(1)}, f32[153,16]{0,1:T(8,128)S(1)}, u32[]{:S(2)}, u32[]{:S(2)}) collective-permute-start(f32[153,16]{0,1:T(8,128)S(1)} %add.154), channel_id=1, source_target_pairs={{4,0},{5,1},{6,2},{7,3},{8,4},{9,5},{10,6},{11,7},{12,8},{13,9},{1... | collective-permute-start | bytes 29384 | tf_op jit(solution)/shard_map/ppermute | solution.py:102
  288.5 8.7 %collective-permute-start.16 = (f32[153,16]{0,1:T(8,128)S(1)}, f32[153,16]{0,1:T(8,128)S(1)}, u32[]{:S(2)}, u32[]{:S(2)}) collective-permute-start(f32[153,16]{0,1:T(8,128)S(1)} %add.155), channel_id=1, source_target_pairs={{8,0},{9,1},{10,2},{11,3},{12,4},{13,5},{14,6},{15,7},{24,16},{25,... | collective-permute-start | bytes 29384 | tf_op jit(solution)/shard_map/ppermute | solution.py:102
  289.9 35.1 %collective-permute-start.12 = (f32[153,1024]{1,0:T(8,128)S(1)}, f32[153,1024]{1,0:T(8,128)S(1)}, u32[]{:S(2)}, u32[]{:S(2)}) collective-permute-start(f32[153,1024]{1,0:T(8,128)S(1)} %add.151), channel_id=1, source_target_pairs={{8,0},{9,1},{10,2},{11,3},{12,4},{13,5},{14,6},{15,7},{24,16},{25,... | collective-permute-start | bytes 1880072 | tf_op jit(solution)/shard_map/ppermute | solution.py:102
  366.3 69.1 %collective-permute-start.17 = (f32[2,2048]{1,0:T(2,128)S(1)}, f32[2,2048]{1,0:T(2,128)S(1)}, u32[]{:S(2)}, u32[]{:S(2)}) collective-permute-start(f32[2,2048]{1,0:T(2,128)S(1)} %pad_add_fusion.1), channel_id=1, source_target_pairs={{1,0},{2,1},{3,2},{4,3},{5,4},{6,5},{7,6},{8,7},{9,8},{10,9},{11,1... | collective-permute-start | bytes 49160 | tf_op jit(solution)/shard_map/ppermute | solution.py:15
  (65 other events, 435.8 us)
Sparse Core Ops, SparseCore 0:
  10.9 64.5 all-gather.1
  209.4 80.7 reduce-scatter.2
  349.3 118.7 reduce-scatter.4
where the time goes:
time: 488 us; the launch traced here: 479 us
  waiting for transfers between devices  193 us (40%)
  matrix products  88.1 us (18%)
  blocking collectives  62 us (13%)
  starting transfers between devices  55.5 us (11%)
  local copies, waits for them, and re-layouts  33.2 us (7%)
  other arithmetic  30.5 us (6%)
  between operations  15.8 us (3%)
    ppermute x16, waiting for transfers between devices, exclusive_scan(): moved = lax.ppermute(total, axis, pairs)  103 us
    unnamed x1, blocking collectives  62 us
    all_gather x1, waiting for transfers between devices, body(): lax.all_gather(jnp.concatenate((w_query, w_key, w_value), axis=1), 'ctx',...  58.3 us
    ppermute x16, starting transfers between devices, exclusive_scan(): moved = lax.ppermute(total, axis, pairs)  51.8 us
    reduce_scatter x1, waiting for transfers between devices, body(): lax.psum_scatter(lax.dot_general(gated, d_kv, (((0,), (0,)), ((), ())), p...  31.7 us
    dot_general x3, matrix products, block_attend(): numer = jnp.einsum('hts,she->the', weight, value, precision=high)  12.7 us
    dot_general x4, matrix products, features(): jnp.einsum('...f,fp->...p', block, jnp.asarray(eye[:, rows]), precision=h...  12.5 us
    dot_general x3, matrix products, block_attend(): jnp.einsum('thn,nhe->the', phi_query, state.reshape(width, heads, hdim),...  12 us
  transfers between devices with their start and end apart: 21, of which 12 were waited for; matrix products, arithmetic and copies ran while one was open for 12% of the time, Pallas kernels for 0%

commit v1 on v0

--- a/solution.py
+++ b/solution.py
@@ -92,17 +92,19 @@
 
 def exclusive_scan(parts, axis, direction):
     count = lax.axis_size(axis)
-    total = parts
+    state, norm = parts
+    joined = jnp.concatenate((state, norm), axis=1)
+    total = joined
     step = 1
     while step < count:
         if direction > 0:
             pairs = [(source, source + step) for source in range(count - step)]
         else:
             pairs = [(source + step, source) for source in range(count - step)]
-        moved = lax.ppermute(total, axis, pairs)
-        total = jax.tree.map(jnp.add, total, moved)
+        total = total + lax.ppermute(total, axis, pairs)
         step *= 2
-    return jax.tree.map(jnp.subtract, total, parts)
+    total = total - joined
+    return (total[:, : state.shape[1]], total[:, state.shape[1] :])
 
 
 def local_gate(tokens_f, rim_f, kernel):

time: 488 us -> 488 us (level)
  waiting for transfers between devices: 193 us -> 225 us
  starting transfers between devices: 55.5 us -> 32.6 us
  other arithmetic: 30.5 us -> 21.2 us
    ppermute x16 -> x8, waiting for transfers between devices: 103 us -> 133 us  [exclusive_scan(): total = total + lax.ppermute(total, axis, pairs)]
    ppermute x16 -> x8, starting transfers between devices: 51.8 us -> 28.9 us  [exclusive_scan(): total = total + lax.ppermute(total, axis, pairs)]
    add x12 -> x6, other arithmetic: 9.07 us -> 3.94 us  [exclusive_scan(): total = total + lax.ppermute(total, axis, pairs)]
  transfers between devices with their start and end apart: 21 -> 13, of which waited for: 12 -> 10; matrix products, arithmetic and copies ran while one was open for 12% -> 9% of each run, Pallas kernels for 0% -> 0%
where the time goes in v1:
time: 488 us; the launch traced here: 478 us
  waiting for transfers between devices  225 us (46%)
  matrix products  90.5 us (19%)
  blocking collectives  62 us (13%)
  starting transfers between devices  32.6 us (7%)
  local copies, waits for them, and re-layouts  31.2 us (6%)
  other arithmetic  21.2 us (4%)
  between operations  15.5 us (3%)
    ppermute x8, waiting for transfers between devices, exclusive_scan(): total = total + lax.ppermute(total, axis, pairs)  133 us
    unnamed x1, blocking collectives  62 us
    all_gather x1, waiting for transfers between devices, body(): lax.all_gather(jnp.concatenate((w_query, w_key, w_value), axis=1), 'ctx',...  58.9 us
    reduce_scatter x1, waiting for transfers between devices, body(): lax.psum_scatter(lax.dot_general(gated, d_kv, (((0,), (0,)), ((), ())), p...  33.7 us
    ppermute x8, starting transfers between devices, exclusive_scan(): total = total + lax.ppermute(total, axis, pairs)  28.9 us
    dot_general x3, matrix products, block_attend(): numer = jnp.einsum('hts,she->the', weight, value, precision=high)  12.9 us
    dot_general x4, matrix products, features(): jnp.einsum('...f,fp->...p', block, jnp.asarray(eye[:, rows]), precision=h...  12.5 us
    dot_general x3, matrix products, block_attend(): jnp.einsum('thn,nhe->the', phi_query, state.reshape(width, heads, hdim),...  11.2 us
  transfers between devices with their start and end apart: 13, of which 10 were waited for; matrix products, arithmetic and copies ran while one was open for 9% of the time, Pallas kernels for 0%

profile of v1, /device:TPU:0, one launch (start us, length us, event | category | flops | bytes accessed | tf_op | source)
XLA Modules:
  0.0 478.3 jit_solution(12053799779798196737)
XLA Ops:
  16.5 58.9 %all-gather.2.cloned.1.call-done = bf16[2048,1536]{1,0:T(8,128)(2,1)} async-done(((bf16[128,1536]{1,0:T(8,128)(2,1)}), bf16[2048,1536]{1,0:T(8,128)(2,1)}) %all-gather.2.cloned.1.call-update) | async-done | bytes 6291472 | tf_op jit(solution)/shard_map/all_gather | solution.py:124
  86.3 6.8 %multiply_multiply_fusion = (f32[256,16,136]{0,2,1:T(8,128)}, f32[256,16,136]{0,2,1:T(8,128)S(1)}, f32[256,16,136]{0,2,1:T(8,128)}) fusion(f32[256,16,136]{0,2,1:T(8,128)} %fusion.97, f32[136]{0:T(256)} %constant.31.clone, f32[256,16,136]{0,2,1:T(8,128)} %fusion.95, f32[256,16,136]{0,2,1:T(8,128)} %fusion.96, bf16[256,16,16]{0,2,1:T(8,128)(2,1)} %bitcast.132, ...), kind=kOutput, calls=%fused_computation.24 | convolution fusion | flops 109182976 | bytes 13509664 | tf_op jit(solution)/shard_map/jvp(...f,fp->...p)/dot_general | solution.py:30
  95.3 4.3 fusion.29
  100.9 4.0 fusion.23
  110.5 11.3 %collective-permute-start.2 = (f32[153,1040]{1,0:T(8,128)S(1)}, f32[153,1040]{1,0:T(8,128)S(1)}, u32[]{:S(2)}, u32[]{:S(2)}) collective-permute-start(f32[153,1040]{1,0:T(8,128)S(1)} %fusion.89), channel_id=1, source_target_pairs={{0,2},{1,3},{2,4},{3,5},{4,6},{5,7},{6,8},{7,9},{8,10},{9,11},{10,... | collective-permute-start | bytes 1909448 | tf_op jit(solution)/shard_map/ppermute | solution.py:104
  121.8 15.9 %collective-permute-done.2 = f32[153,1040]{1,0:T(8,128)S(1)} collective-permute-done((f32[153,1040]{1,0:T(8,128)S(1)}, f32[153,1040]{1,0:T(8,128)S(1)}, u32[]{:S(2)}, u32[]{:S(2)}) %collective-permute-start.2) | collective-permute-done | bytes 636512 | tf_op jit(solution)/shard_map/ppermute | solution.py:104
  138.6 5.4 %collective-permute-start.3 = (f32[153,1040]{1,0:T(8,128)}, f32[153,1040]{1,0:T(8,128)}, u32[]{:S(2)}, u32[]{:S(2)}) collective-permute-start(f32[153,1040]{1,0:T(8,128)} %add.112), channel_id=1, source_target_pairs={{0,4},{1,5},{2,6},{3,7},{4,8},{5,9},{6,10},{7,11},{8,12},{9,13},{1... | collective-permute-start | bytes 1909448 | tf_op jit(solution)/shard_map/ppermute | solution.py:104
  148.7 7.5 %collective-permute-done.3 = f32[153,1040]{1,0:T(8,128)} collective-permute-done((f32[153,1040]{1,0:T(8,128)}, f32[153,1040]{1,0:T(8,128)}, u32[]{:S(2)}, u32[]{:S(2)}) %collective-permute-start.3) | collective-permute-done | bytes 636512 | tf_op jit(solution)/shard_map/ppermute | solution.py:104
  157.6 4.7 collective-permute-start.4
  165.2 3.6 fusion.53
  168.8 4.7 collective-permute-done.4
  180.9 4.2 multiply_reduce_fusion.4
  186.5 4.0 fusion.59
  190.5 3.7 fusion.1
  204.5 4.0 fusion.73
  218.5 20.7 %collective-permute-done.6 = f32[153,1040]{1,0:T(8,128)S(1)} collective-permute-done((f32[153,1040]{1,0:T(8,128)S(1)}, f32[153,1040]{1,0:T(8,128)S(1)}, u32[]{:S(2)}, u32[]{:S(2)}) %collective-permute-start.6) | collective-permute-done | bytes 636512 | tf_op jit(solution)/shard_map/ppermute | solution.py:104
  240.6 46.7 %collective-permute-done.7 = f32[153,1040]{1,0:T(8,128)S(1)} collective-permute-done((f32[153,1040]{1,0:T(8,128)S(1)}, f32[153,1040]{1,0:T(8,128)S(1)}, u32[]{:S(2)}, u32[]{:S(2)}) %collective-permute-start.7) | collective-permute-done | bytes 636512 | tf_op jit(solution)/shard_map/ppermute | solution.py:104
  288.7 5.7 %fusion.51 = f32[16,64,256]{2,1,0:T(8,128)} fusion(f32[16,256,256]{1,2,0:T(8,128)S(1)} %copy-done.63, pred[256,256]{0,1:T(8,128)(4,1)S(1)} %copy-done.53, f32[256,16,64]{0,2,1:T(8,128)S(1)} %copy-done.16), kind=kOutput, calls=%fused_computation.66 | convolution fusion | flops 811597824 | bytes 6356992 | tf_op jit(solution)/shard_map/transpose(jvp(hts,she->the))/dot_general | solution.py:48
  294.4 32.3 %collective-permute-done.8 = f32[153,1040]{1,0:T(8,128)S(1)} collective-permute-done((f32[153,1040]{1,0:T(8,128)S(1)}, f32[153,1040]{1,0:T(8,128)S(1)}, u32[]{:S(2)}, u32[]{:S(2)}) %collective-permute-start.8) | collective-permute-done | bytes 636512 | tf_op jit(solution)/shard_map/ppermute | solution.py:104
  343.6 5.5 %fusion.63 = f32[2048,1280]{1,0:T(8,128)} fusion(bf16[256,2048]{1,0:T(8,128)(2,1)S(1)} %copy-done.12, bf16[256,1024]{0,1:T(8,128)(2,1)S(1)} %bitcast.140, bf16[256,256]{0,1:T(8,128)(2,1)S(1)} %bitcast.151), kind=kOutput, calls=%fused_computation.90 | convolution fusion | flops 1343488000 | bytes 12189696 | tf_op jit(solution)/shard_map/dot_general | solution.py:153
  352.0 4.2 fusion.2
  356.3 4.9 %multiply_reduce_fusion.2 = (f32[2048]{0:T(1024)S(1)}, f32[2048]{0:T(1024)S(1)}, f32[2048]{0:T(1024)S(1)}, f32[256,2048]{1,0:T(8,128)S(1)}, f32[256,2048]{1,0:T(8,128)}) fusion(f32[256,2048]{1,0:T(8,128)S(1)} %copy-done.6, f32[2,2048]{1,0:T(2,128)S(1)} %copy-done.43, bf16[256,2048]{1,0:T(8,128)(2,1)S(1)} %copy-done.14, f32[256,2048]{1,0:T(8,128)S(1)} %fusion.2, ...), kind=kOutput, calls=%fused_computation.37 | convolution fusion | flops 544729088 | bytes 11837440 | tf_op jit(solution)/shard_map/dot_general | solution.py:159
  365.4 62.0 %all-reduce.6 = f32[48,128]{1,0:T(8,128)S(1)} all-reduce(f32[48,128]{1,0:T(8,128)S(1)} %reshape.119), channel_id=4, replica_groups=mesh['groups'=2,'ctx'=16] {'ctx'}, use_global_device_ids=true, to_apply=%region_10.11.clone | all-reduce | flops 6144 | bytes 49152
  434.4 33.7 %reduce-scatter.5.cloned.1.call-done = f32[128,1280]{1,0:T(8,128)} async-done(((f32[2048,1280]{1,0:T(8,128)}), f32[128,1280]{1,0:T(8,128)}) %reduce-scatter.5.cloned.1.call-update) | async-done | bytes 655376 | tf_op jit(solution)/shard_map/reduce_scatter | solution.py:152
  (221 shorter events, 104.3 us)
Async XLA Ops:
  7.2 68.3 %all-gather.2.cloned.1.call-start = ((), (), s32[]{:S(2)}) async-start(), calls=%async_computation.2 | async-start | bytes 6684672 | tf_op jit(solution)/shard_map/all_gather | solution.py:124
  9.0 318.6 %reduce-scatter.3.cloned.1.call-start = ((), (), s32[]{:S(2)}) async-start(), calls=%async_computation.3 | async-start | bytes 2228224 | tf_op jit(solution)/shard_map/reduce_scatter | solution.py:144
  9.9 5.4 %collective-permute-start = (bf16[2,2048]{1,0:T(2,128)(2,1)S(1)}, bf16[2,2048]{1,0:T(2,128)(2,1)S(1)}, u32[]{:S(2)}, u32[]{:S(2)}) collective-permute-start(bf16[2,2048]{1,0:T(2,128)(2,1)S(1)} %slice.64), channel_id=1, source_target_pairs={{0,1},{1,2},{2,3},{3,4},{4,5},{5,6},{6,7},{7,8},{8,9},{9,10},{10,1... | collective-permute-start | bytes 24584 | tf_op jit(solution)/shard_map/ppermute | solution.py:15
  14.6 63.1 %copy-start.5 = (f32[256,2048]{1,0:T(8,128)}, f32[256,2048]{1,0:T(8,128)S(1)}, u32[]{:S(2)}) copy-start(f32[256,2048]{1,0:T(8,128)S(1)} %convert_element_type.51) | copy-start | bytes 6291460
  15.3 60.2 %copy-start.42 = (f32[2,2048]{1,0:T(2,128)}, f32[2,2048]{1,0:T(2,128)S(1)}, u32[]{:S(2)}) copy-start(f32[2,2048]{1,0:T(2,128)S(1)} %convert_element_type.52) | copy-start | bytes 49156
  16.5 78.8 %copy-start.10 = (bf16[256,2048]{1,0:T(8,128)(2,1)}, bf16[256,2048]{1,0:T(8,128)(2,1)S(1)}, u32[]{:S(2)}) copy-start(bf16[256,2048]{1,0:T(8,128)(2,1)S(1)} %add_convert_fusion) | copy-start | bytes 3145732
  16.5 62.3 %copy-start.38 = (f32[16,136,1]{1,0,2:T(8,128)S(1)}, f32[16,136,1]{1,0,2:T(8,128)}, u32[]{:S(2)}) copy-start(f32[16,136,1]{1,0,2:T(8,128)} %constant.51) | copy-start | bytes 26116
  95.3 15.1 %copy-start.33 = (f32[153,16]{1,0:T(8,128)}, f32[153,16]{1,0:T(8,128)S(1)}, u32[]{:S(2)}) copy-start(f32[153,16]{1,0:T(8,128)S(1)} %copy.97) | copy-start | bytes 29380
  100.9 89.6 %copy-start.19 = (bf16[256,1024]{0,1:T(8,128)(2,1)}, bf16[256,1024]{0,1:T(8,128)(2,1)S(1)}, u32[]{:S(2)}) copy-start(bf16[256,1024]{0,1:T(8,128)(2,1)S(1)} %copy.91) | copy-start | bytes 1572868
  106.4 4.0 collective-permute-start.1
  110.5 27.2 %collective-permute-start.2 = (f32[153,1040]{1,0:T(8,128)S(1)}, f32[153,1040]{1,0:T(8,128)S(1)}, u32[]{:S(2)}, u32[]{:S(2)}) collective-permute-start(f32[153,1040]{1,0:T(8,128)S(1)} %fusion.89), channel_id=1, source_target_pairs={{0,2},{1,3},{2,4},{3,5},{4,6},{5,7},{6,8},{7,9},{8,10},{9,11},{10,... | collective-permute-start | bytes 1909448 | tf_op jit(solution)/shard_map/ppermute | solution.py:104
  138.6 23.7 %copy-start.26 = (bf16[256,256]{0,1:T(8,128)(2,1)S(1)}, bf16[256,256]{0,1:T(8,128)(2,1)}, u32[]{:S(2)}) copy-start(bf16[256,256]{0,1:T(8,128)(2,1)} %copy-done.25) | copy-start | bytes 393220
  138.6 17.5 %collective-permute-start.3 = (f32[153,1040]{1,0:T(8,128)}, f32[153,1040]{1,0:T(8,128)}, u32[]{:S(2)}, u32[]{:S(2)}) collective-permute-start(f32[153,1040]{1,0:T(8,128)} %add.112), channel_id=1, source_target_pairs={{0,4},{1,5},{2,6},{3,7},{4,8},{5,9},{6,10},{7,11},{8,12},{9,13},{1... | collective-permute-start | bytes 1909448 | tf_op jit(solution)/shard_map/ppermute | solution.py:104
  157.6 15.9 %collective-permute-start.4 = (f32[153,1040]{1,0:T(8,128)S(1)}, f32[153,1040]{1,0:T(8,128)S(1)}, u32[]{:S(2)}, u32[]{:S(2)}) collective-permute-start(f32[153,1040]{1,0:T(8,128)S(1)} %add.113), channel_id=1, source_target_pairs={{0,8},{1,9},{2,10},{3,11},{4,12},{5,13},{6,14},{7,15},{16,24},{17,... | collective-permute-start | bytes 1909448 | tf_op jit(solution)/shard_map/ppermute | solution.py:104
  165.2 8.3 %copy-start.34 = (f32[153,16]{1,0:T(8,128)S(1)}, f32[153,16]{1,0:T(8,128)}, u32[]{:S(2)}) copy-start(f32[153,16]{1,0:T(8,128)} %copy-done.33) | copy-start | bytes 29380
  211.3 4.4 collective-permute-start.5
  212.6 255.5 %reduce-scatter.5.cloned.1.call-start = ((), (), s32[]{:S(2)}) async-start(), calls=%async_computation.4 | async-start | bytes 11141120 | tf_op jit(solution)/shard_map/reduce_scatter | solution.py:152
  215.7 73.0 %copy-start.63 = (f32[16,256,256]{1,2,0:T(8,128)S(1)}, f32[16,256,256]{1,2,0:T(8,128)}, u32[]{:S(2)}) copy-start(f32[16,256,256]{1,2,0:T(8,128)} %copy-done.61) | copy-start | bytes 12582916
  217.1 71.6 %copy-start.16 = (f32[256,16,64]{0,2,1:T(8,128)S(1)}, f32[256,16,64]{0,2,1:T(8,128)}, u32[]{:S(2)}) copy-start(f32[256,16,64]{0,2,1:T(8,128)} %copy-done.15) | copy-start | bytes 3145732
  217.1 71.6 %copy-start.53 = (pred[256,256]{0,1:T(8,128)(4,1)S(1)}, pred[256,256]{0,1:T(8,128)(4,1)}, u32[]{:S(2)}) copy-start(pred[256,256]{0,1:T(8,128)(4,1)} %iota_compare_fusion) | copy-start | bytes 196612
  217.1 22.1 %collective-permute-start.6 = (f32[153,1040]{1,0:T(8,128)S(1)}, f32[153,1040]{1,0:T(8,128)S(1)}, u32[]{:S(2)}, u32[]{:S(2)}) collective-permute-start(f32[153,1040]{1,0:T(8,128)S(1)} %fusion.88), channel_id=1, source_target_pairs={{2,0},{3,1},{4,2},{5,3},{6,4},{7,5},{8,6},{9,7},{10,8},{11,9},{12,... | collective-permute-start | bytes 1909448 | tf_op jit(solution)/shard_map/ppermute | solution.py:104
  239.3 48.0 %collective-permute-start.7 = (f32[153,1040]{1,0:T(8,128)S(1)}, f32[153,1040]{1,0:T(8,128)S(1)}, u32[]{:S(2)}, u32[]{:S(2)}) collective-permute-start(f32[153,1040]{1,0:T(8,128)S(1)} %add.122), channel_id=1, source_target_pairs={{4,0},{5,1},{6,2},{7,3},{8,4},{9,5},{10,6},{11,7},{12,8},{13,9},{1... | collective-permute-start | bytes 1909448 | tf_op jit(solution)/shard_map/ppermute | solution.py:104
  287.4 39.3 %collective-permute-start.8 = (f32[153,1040]{1,0:T(8,128)S(1)}, f32[153,1040]{1,0:T(8,128)S(1)}, u32[]{:S(2)}, u32[]{:S(2)}) collective-permute-start(f32[153,1040]{1,0:T(8,128)S(1)} %add.123), channel_id=1, source_target_pairs={{8,0},{9,1},{10,2},{11,3},{12,4},{13,5},{14,6},{15,7},{24,16},{25,... | collective-permute-start | bytes 1909448 | tf_op jit(solution)/shard_map/ppermute | solution.py:104
  364.1 69.2 %collective-permute-start.9 = (f32[2,2048]{1,0:T(2,128)S(1)}, f32[2,2048]{1,0:T(2,128)S(1)}, u32[]{:S(2)}, u32[]{:S(2)}) collective-permute-start(f32[2,2048]{1,0:T(2,128)S(1)} %pad_add_fusion.1), channel_id=1, source_target_pairs={{1,0},{2,1},{3,2},{4,3},{5,4},{6,5},{7,6},{8,7},{9,8},{10,9},{11,1... | collective-permute-start | bytes 49160 | tf_op jit(solution)/shard_map/ppermute | solution.py:15
  (53 other events, 200.9 us)
Sparse Core Ops, SparseCore 0:
  10.9 64.5 all-gather.1
  212.7 100.3 reduce-scatter.2
  349.2 118.8 reduce-scatter.4

commit v2 on v1

--- a/solution.py
+++ b/solution.py
@@ -140,10 +140,9 @@
     query_part = lax.dot_general(
         gated, d_query, (((0,), (0,)), ((), ())), preferred_element_type=jnp.float32
     )
-    query_part, d_state, d_norm = lax.optimization_barrier((query_part, d_state, d_norm))
+    later_state, later_norm = exclusive_scan((d_state, d_norm), "ctx", -1)
+    query_part, later_state, later_norm = lax.optimization_barrier((query_part, later_state, later_norm))
     grad_query = lax.psum_scatter(query_part, "ctx", scatter_dimension=0, tiled=True)
-    later_state, later_norm = exclusive_scan((d_state, d_norm), "ctx", -1)
-    later_state, later_norm, grad_query = lax.optimization_barrier((later_state, later_norm, grad_query))
     _, back_state = jax.vjp(block_state, key_f, value_f)
     extra_key, extra_value = back_state((later_state, later_norm))
     d_key = (d_key + extra_key).reshape(length, qk_cols).astype(jnp.bfloat16)

time: 488 us -> 518 us (1.061)
  waiting for transfers between devices: 225 us -> 261 us
  matrix products: 90.5 us -> 83.9 us
    reduce_scatter x1, waiting for transfers between devices: 0.01 us -> 62.3 us  [body(): lax.psum_scatter(query_part, 'ctx', scatter_dimension=0, tiled=True)]
    ppermute x8, waiting for transfers between devices: 133 us -> 106 us  [exclusive_scan(): total = total + lax.ppermute(total, axis, pairs)]
  transfers between devices with their start and end apart: 13 -> 13, of which waited for: 10 -> 10; matrix products, arithmetic and copies ran while one was open for 9% -> 12% of each run, Pallas kernels for 0% -> 0%
where the time goes in v2:
time: 518 us; the launch traced here: 509 us
  waiting for transfers between devices  261 us (50%)
  matrix products  83.9 us (16%)
  blocking collectives  62.1 us (12%)
  starting transfers between devices  32.7 us (6%)
  local copies, waits for them, and re-layouts  28.6 us (6%)
  other arithmetic  25.4 us (5%)
  between operations  15.7 us (3%)
    ppermute x8, waiting for transfers between devices, exclusive_scan(): total = total + lax.ppermute(total, axis, pairs)  106 us
    reduce_scatter x1, waiting for transfers between devices, body(): lax.psum_scatter(query_part, 'ctx', scatter_dimension=0, tiled=True)  62.3 us
    unnamed x1, blocking collectives  62.1 us
    all_gather x1, waiting for transfers between devices, body(): lax.all_gather(jnp.concatenate((w_query, w_key, w_value), axis=1), 'ctx',...  58.3 us
    reduce_scatter x1, waiting for transfers between devices, body(): lax.psum_scatter(lax.dot_general(gated, d_kv, (((0,), (0,)), ((), ())), p...  34 us
    ppermute x8, starting transfers between devices, exclusive_scan(): total = total + lax.ppermute(total, axis, pairs)  28.9 us
    dot_general x3, matrix products, block_attend(): numer = jnp.einsum('hts,she->the', weight, value, precision=high)  15 us
    dot_general x3, matrix products, block_attend(): jnp.einsum('thn,nhe->the', phi_query, state.reshape(width, heads, hdim),...  13.3 us
  transfers between devices with their start and end apart: 13, of which 10 were waited for; matrix products, arithmetic and copies ran while one was open for 12% of the time, Pallas kernels for 0%

profile of v2, /device:TPU:0, one launch (start us, length us, event | category | flops | bytes accessed | tf_op | source)
XLA Modules:
  0.0 509.0 jit_solution(4823266002960201978)
XLA Ops:
  17.2 58.3 %all-gather.2.cloned.1.call-done = bf16[2048,1536]{1,0:T(8,128)(2,1)} async-done(((bf16[128,1536]{1,0:T(8,128)(2,1)}), bf16[2048,1536]{1,0:T(8,128)(2,1)}) %all-gather.2.cloned.1.call-update) | async-done | bytes 6291472 | tf_op jit(solution)/shard_map/all_gather | solution.py:124
  78.9 3.5 fusion.29
  86.0 3.7 multiply_multiply_fusion
  101.6 11.3 %collective-permute-start.2 = (f32[153,1040]{1,0:T(8,128)S(1)}, f32[153,1040]{1,0:T(8,128)S(1)}, u32[]{:S(2)}, u32[]{:S(2)}) collective-permute-start(f32[153,1040]{1,0:T(8,128)S(1)} %fusion.89), channel_id=1, source_target_pairs={{0,2},{1,3},{2,4},{3,5},{4,6},{5,7},{6,8},{7,9},{8,10},{9,11},{10,... | collective-permute-start | bytes 1909448 | tf_op jit(solution)/shard_map/ppermute | solution.py:104
  112.9 15.9 %collective-permute-done.2 = f32[153,1040]{1,0:T(8,128)S(1)} collective-permute-done((f32[153,1040]{1,0:T(8,128)S(1)}, f32[153,1040]{1,0:T(8,128)S(1)}, u32[]{:S(2)}, u32[]{:S(2)}) %collective-permute-start.2) | collective-permute-done | bytes 636512 | tf_op jit(solution)/shard_map/ppermute | solution.py:104
  129.7 5.2 %collective-permute-start.3 = (f32[153,1040]{1,0:T(8,128)}, f32[153,1040]{1,0:T(8,128)}, u32[]{:S(2)}, u32[]{:S(2)}) collective-permute-start(f32[153,1040]{1,0:T(8,128)} %add.112), channel_id=1, source_target_pairs={{0,4},{1,5},{2,6},{3,7},{4,8},{5,9},{6,10},{7,11},{8,12},{9,13},{1... | collective-permute-start | bytes 1909448 | tf_op jit(solution)/shard_map/ppermute | solution.py:104
  139.6 7.5 %collective-permute-done.3 = f32[153,1040]{1,0:T(8,128)} collective-permute-done((f32[153,1040]{1,0:T(8,128)}, f32[153,1040]{1,0:T(8,128)}, u32[]{:S(2)}, u32[]{:S(2)}) %collective-permute-start.3) | collective-permute-done | bytes 636512 | tf_op jit(solution)/shard_map/ppermute | solution.py:104
  148.5 4.7 collective-permute-start.4
  156.1 3.5 fusion.53
  159.7 4.8 collective-permute-done.4
  167.3 3.4 fusion.90
  170.8 4.2 multiply_reduce_fusion.4
  178.7 4.4 fusion.59
  187.9 4.8 add_bitcast_fusion.1
  200.5 13.1 %collective-permute-done.6 = f32[153,1040]{1,0:T(8,128)S(1)} collective-permute-done((f32[153,1040]{1,0:T(8,128)S(1)}, f32[153,1040]{1,0:T(8,128)S(1)}, u32[]{:S(2)}, u32[]{:S(2)}) %collective-permute-start.6) | collective-permute-done | bytes 636512 | tf_op jit(solution)/shard_map/ppermute | solution.py:104
  218.0 36.9 %collective-permute-done.7 = f32[153,1040]{1,0:T(8,128)S(1)} collective-permute-done((f32[153,1040]{1,0:T(8,128)S(1)}, f32[153,1040]{1,0:T(8,128)S(1)}, u32[]{:S(2)}, u32[]{:S(2)}) %collective-permute-start.7) | collective-permute-done | bytes 636512 | tf_op jit(solution)/shard_map/ppermute | solution.py:104
  259.1 8.2 %fusion.51 = f32[16,64,256]{2,1,0:T(8,128)} fusion(f32[16,256,256]{1,2,0:T(8,128)} %copy-done.62, pred[256,256]{0,1:T(8,128)(4,1)S(1)} %copy-done.54, f32[256,16,64]{0,2,1:T(8,128)} %copy-done.18), kind=kOutput, calls=%fused_computation.66 | convolution fusion | flops 811597824 | bytes 6356992 | tf_op jit(solution)/shard_map/transpose(jvp(hts,she->the))/dot_general | solution.py:48
  267.3 26.1 %collective-permute-done.8 = f32[153,1040]{1,0:T(8,128)} collective-permute-done((f32[153,1040]{1,0:T(8,128)}, f32[153,1040]{1,0:T(8,128)}, u32[]{:S(2)}, u32[]{:S(2)}) %collective-permute-start.8) | collective-permute-done | bytes 636512 | tf_op jit(solution)/shard_map/ppermute | solution.py:104
  309.8 5.6 %fusion.63 = f32[2048,1280]{1,0:T(8,128)} fusion(bf16[256,2048]{1,0:T(8,128)(2,1)S(1)} %copy-done.15, bf16[256,1024]{0,1:T(8,128)(2,1)S(1)} %bitcast.140, bf16[256,256]{0,1:T(8,128)(2,1)S(1)} %bitcast.151), kind=kOutput, calls=%fused_computation.90 | convolution fusion | flops 1343488000 | bytes 12189696 | tf_op jit(solution)/shard_map/dot_general | solution.py:152
  318.4 3.6 fusion.2
  322.1 5.3 %multiply_reduce_fusion.2 = (f32[2048]{0:T(1024)S(1)}, f32[2048]{0:T(1024)S(1)}, f32[2048]{0:T(1024)S(1)}, f32[256,2048]{1,0:T(8,128)}, f32[256,2048]{1,0:T(8,128)}) fusion(f32[256,2048]{1,0:T(8,128)S(1)} %copy-done.9, f32[2,2048]{1,0:T(2,128)S(1)} %copy-done.44, bf16[256,2048]{1,0:T(8,128)(2,1)S(1)} %copy-done.17, f32[256,2048]{1,0:T(8,128)S(1)} %fusion.2, ...), kind=kOutput, calls=%fused_computation.37 | convolution fusion | flops 544729088 | bytes 11837440 | tf_op jit(solution)/shard_map/dot_general | solution.py:158
  333.5 62.1 %all-reduce.6 = f32[48,128]{1,0:T(8,128)S(1)} all-reduce(f32[48,128]{1,0:T(8,128)S(1)} %reshape.119), channel_id=4, replica_groups=mesh['groups'=2,'ctx'=16] {'ctx'}, use_global_device_ids=true, to_apply=%region_10.11.clone | all-reduce | flops 6144 | bytes 49152
  402.5 34.0 %reduce-scatter.5.cloned.1.call-done = f32[128,1280]{1,0:T(8,128)} async-done(((f32[2048,1280]{1,0:T(8,128)}), f32[128,1280]{1,0:T(8,128)}) %reduce-scatter.5.cloned.1.call-update) | async-done | bytes 655376 | tf_op jit(solution)/shard_map/reduce_scatter | solution.py:151
  440.0 62.3 %reduce-scatter.3.cloned.1.call-done = f32[128,256]{1,0:T(8,128)} async-done(((f32[2048,256]{1,0:T(8,128)}), f32[128,256]{1,0:T(8,128)}) %reduce-scatter.3.cloned.1.call-update) | async-done | bytes 131088 | tf_op jit(solution)/shard_map/reduce_scatter | solution.py:145
  (221 shorter events, 101.0 us)
Async XLA Ops:
  7.2 8.8 %copy-start.16 = (bf16[256,2048]{1,0:T(8,128)(2,1)S(1)}, bf16[256,2048]{1,0:T(8,128)(2,1)}, u32[]{:S(2)}) copy-start(bf16[256,2048]{1,0:T(8,128)(2,1)} %param.15) | copy-start | bytes 3145732
  7.2 68.3 %all-gather.2.cloned.1.call-start = ((), (), s32[]{:S(2)}) async-start(), calls=%async_computation.2 | async-start | bytes 6684672 | tf_op jit(solution)/shard_map/all_gather | solution.py:124
  9.1 427.5 %reduce-scatter.5.cloned.1.call-start = ((), (), s32[]{:S(2)}) async-start(), calls=%async_computation.4 | async-start | bytes 11141120 | tf_op jit(solution)/shard_map/reduce_scatter | solution.py:151
  9.9 4.8 collective-permute-start
  14.7 76.6 %copy-start.55 = (f32[153]{0:T(256)}, f32[153]{0:T(256)S(1)}, u32[]{:S(2)}) copy-start(f32[153]{0:T(256)S(1)} %pad.37.clone) | copy-start | bytes 1840
  17.1 61.7 %copy-start.13 = (bf16[256,2048]{1,0:T(8,128)(2,1)}, bf16[256,2048]{1,0:T(8,128)(2,1)S(1)}, u32[]{:S(2)}) copy-start(bf16[256,2048]{1,0:T(8,128)(2,1)S(1)} %add_convert_fusion) | copy-start | bytes 3145732
  78.7 74.5 %copy-start.27 = (bf16[256,256]{0,1:T(8,128)(2,1)}, bf16[256,256]{0,1:T(8,128)(2,1)S(1)}, u32[]{:S(2)}) copy-start(bf16[256,256]{0,1:T(8,128)(2,1)S(1)} %copy.92) | copy-start | bytes 393220
  78.9 12.4 %copy-start.24 = (f32[256,256]{0,1:T(8,128)}, f32[256,256]{0,1:T(8,128)S(1)}, u32[]{:S(2)}) copy-start(f32[256,256]{0,1:T(8,128)S(1)} %copy.95) | copy-start | bytes 786436
  82.7 114.5 %copy-start.22 = (bf16[256,1024]{0,1:T(8,128)(2,1)}, bf16[256,1024]{0,1:T(8,128)(2,1)S(1)}, u32[]{:S(2)}) copy-start(bf16[256,1024]{0,1:T(8,128)(2,1)S(1)} %copy.91) | copy-start | bytes 1572868
  96.6 4.0 collective-permute-start.1
  101.6 27.2 %collective-permute-start.2 = (f32[153,1040]{1,0:T(8,128)S(1)}, f32[153,1040]{1,0:T(8,128)S(1)}, u32[]{:S(2)}, u32[]{:S(2)}) collective-permute-start(f32[153,1040]{1,0:T(8,128)S(1)} %fusion.89), channel_id=1, source_target_pairs={{0,2},{1,3},{2,4},{3,5},{4,6},{5,7},{6,8},{7,9},{8,10},{9,11},{10,... | collective-permute-start | bytes 1909448 | tf_op jit(solution)/shard_map/ppermute | solution.py:104
  129.7 17.4 %collective-permute-start.3 = (f32[153,1040]{1,0:T(8,128)}, f32[153,1040]{1,0:T(8,128)}, u32[]{:S(2)}, u32[]{:S(2)}) collective-permute-start(f32[153,1040]{1,0:T(8,128)} %add.112), channel_id=1, source_target_pairs={{0,4},{1,5},{2,6},{3,7},{4,8},{5,9},{6,10},{7,11},{8,12},{9,13},{1... | collective-permute-start | bytes 1909448 | tf_op jit(solution)/shard_map/ppermute | solution.py:104
  148.5 15.9 %collective-permute-start.4 = (f32[153,1040]{1,0:T(8,128)S(1)}, f32[153,1040]{1,0:T(8,128)S(1)}, u32[]{:S(2)}, u32[]{:S(2)}) collective-permute-start(f32[153,1040]{1,0:T(8,128)S(1)} %add.113), channel_id=1, source_target_pairs={{0,8},{1,9},{2,10},{3,11},{4,12},{5,13},{6,14},{7,15},{16,24},{17,... | collective-permute-start | bytes 1909448 | tf_op jit(solution)/shard_map/ppermute | solution.py:104
  185.6 7.0 %collective-permute-start.5 = (f32[153,1040]{1,0:T(8,128)}, f32[153,1040]{1,0:T(8,128)}, u32[]{:S(2)}, u32[]{:S(2)}) collective-permute-start(f32[153,1040]{1,0:T(8,128)} %pad_maximum_fusion.11), channel_id=1, source_target_pairs={{1,0},{2,1},{3,2},{4,3},{5,4},{6,5},{7,6},{8,7},{9,8},{10,9},{11,1... | collective-permute-start | bytes 1909448 | tf_op jit(solution)/shard_map/ppermute | solution.py:104
  194.1 19.5 %collective-permute-start.6 = (f32[153,1040]{1,0:T(8,128)S(1)}, f32[153,1040]{1,0:T(8,128)S(1)}, u32[]{:S(2)}, u32[]{:S(2)}) collective-permute-start(f32[153,1040]{1,0:T(8,128)S(1)} %fusion.88), channel_id=1, source_target_pairs={{2,0},{3,1},{4,2},{5,3},{6,4},{7,5},{8,6},{9,7},{10,8},{11,9},{12,... | collective-permute-start | bytes 1909448 | tf_op jit(solution)/shard_map/ppermute | solution.py:104
  197.2 17.7 %copy-start.21 = (f32[256,16,136]{0,2,1:T(8,128)S(1)}, f32[256,16,136]{0,2,1:T(8,128)}, u32[]{:S(2)}) copy-start(f32[256,16,136]{0,2,1:T(8,128)} %get-tuple-element.71) | copy-start | bytes 6684676
  200.5 16.1 %copy-start.11 = (f32[16,256,256]{1,2,0:T(8,128)}, f32[16,256,256]{1,2,0:T(8,128)S(1)}, u32[]{:S(2)}) copy-start(f32[16,256,256]{1,2,0:T(8,128)S(1)} %fusion.1) | copy-start | bytes 12582916
  213.6 41.3 %collective-permute-start.7 = (f32[153,1040]{1,0:T(8,128)S(1)}, f32[153,1040]{1,0:T(8,128)S(1)}, u32[]{:S(2)}, u32[]{:S(2)}) collective-permute-start(f32[153,1040]{1,0:T(8,128)S(1)} %add.122), channel_id=1, source_target_pairs={{4,0},{5,1},{6,2},{7,3},{8,4},{9,5},{10,6},{11,7},{12,8},{13,9},{1... | collective-permute-start | bytes 1909448 | tf_op jit(solution)/shard_map/ppermute | solution.py:104
  218.0 41.1 %copy-start.37 = (bf16[256,16,16]{0,2,1:T(8,128)(2,1)}, bf16[256,16,16]{0,2,1:T(8,128)(2,1)S(1)}, u32[]{:S(2)}) copy-start(bf16[256,16,16]{0,2,1:T(8,128)(2,1)S(1)} %fusion.49) | copy-start | bytes 393220
  218.0 39.3 %copy-start.14 = (bf16[256,2048]{1,0:T(8,128)(2,1)S(1)}, bf16[256,2048]{1,0:T(8,128)(2,1)}, u32[]{:S(2)}) copy-start(bf16[256,2048]{1,0:T(8,128)(2,1)} %copy-done.13) | copy-start | bytes 3145732
  218.0 41.1 %copy-start.54 = (pred[256,256]{0,1:T(8,128)(4,1)S(1)}, pred[256,256]{0,1:T(8,128)(4,1)}, u32[]{:S(2)}) copy-start(pred[256,256]{0,1:T(8,128)(4,1)} %iota_compare_fusion) | copy-start | bytes 196612
  255.9 37.5 %collective-permute-start.8 = (f32[153,1040]{1,0:T(8,128)}, f32[153,1040]{1,0:T(8,128)}, u32[]{:S(2)}, u32[]{:S(2)}) collective-permute-start(f32[153,1040]{1,0:T(8,128)} %add.123), channel_id=1, source_target_pairs={{8,0},{9,1},{10,2},{11,3},{12,4},{13,5},{14,6},{15,7},{24,16},{25,... | collective-permute-start | bytes 1909448 | tf_op jit(solution)/shard_map/ppermute | solution.py:104
  315.5 186.8 %reduce-scatter.3.cloned.1.call-start = ((), (), s32[]{:S(2)}) async-start(), calls=%async_computation.3 | async-start | bytes 2228224 | tf_op jit(solution)/shard_map/reduce_scatter | solution.py:145
  332.2 69.2 %collective-permute-start.9 = (f32[2,2048]{1,0:T(2,128)S(1)}, f32[2,2048]{1,0:T(2,128)S(1)}, u32[]{:S(2)}, u32[]{:S(2)}) collective-permute-start(f32[2,2048]{1,0:T(2,128)S(1)} %pad_add_fusion.1), channel_id=1, source_target_pairs={{1,0},{2,1},{3,2},{4,3},{5,4},{6,5},{7,6},{8,7},{9,8},{10,9},{11,1... | collective-permute-start | bytes 49160 | tf_op jit(solution)/shard_map/ppermute | solution.py:15
  (53 other events, 191.5 us)
Sparse Core Ops, SparseCore 0:
  10.9 64.5 all-gather.1
  315.6 120.8 reduce-scatter.4
  440.9 61.3 reduce-scatter.2
